TPU v7x, 256 devices: a whole 4x4x8 slice. The times are simulated.
256 devices in a mesh: tile: 16 (over z, x_lo), obj: 16 (over x_hi, y, core).
Axes of the slice: x: 4 (x_hi: 2, x_lo: 2; x = x_hi * 2 + x_lo), y: 4, z: 8, core: 2. Of those that a mesh axis runs over, the one named last changes fastest.
Arguments:
- adjoint_in: float32 [256, 2, 256, 1024], P('obj', None, 'tile'), may hold values from -6 to 6
- checkpoint_store: float32 [64, 2, 256, 1024], P('obj', None, 'tile'), may hold values from 1900 to 2500, as said below
- interval: int32 [1], replicated, may hold values from 0 to 63
- sea_mask: int32 [256, 1024], P('tile'), may hold values 0 or 1
- zonal_speed: float32 [256, 1024], P('tile'), may hold values from -0.45 to 0.45
- mixing: float32 [256, 1024], P('tile'), may hold values from 0.02 to 0.2
- piston: float32 [256, 32], P('tile'), may hold values from 0.1 to 0.9
- cell_area: float32 [256, 32], P('tile'), may hold values from 5 to 50
- region: int32 [256, 32], P('tile'), may hold values from 0 to 255
Outputs:
- adjoint_out: float32 [256, 2, 256, 1024], P('obj', None, 'tile')
Inputs may be any that keep to these rules, and one draw needn't show every extreme that they name: region numbers name objectives. `checkpoint_store`: dissolved carbon lies in 1900 to 2100 and alkalinity exceeds it by 200 to 400 in every cell.
All inputs are finite; a program needn't handle non-finite values. No bound on the sum of `sea_mask` on one device may be relied on, other than what follows from the above.
Results may differ from a plain program's by a relative error of at most 0.0003.
Values sent between devices are 32-bit elements; how exact they have to be, the bound alone decides.
No kernel may reach another device: no remote copies, remote signals or barrier semaphores. Data moves between devices by JAX's collectives and lax.ppermute only.
A program may use at most 64 MiB of HBM per device.

v0:
```python
import jax
import jax.numpy as jnp
from jax import lax
from jax.sharding import PartitionSpec as P

ROWS = 32
LEVELS = 32
NEWTON = 4
DISSOCIATION_ONE = 1400.0
DISSOCIATION_TWO = 1.1
BORATE_CONSTANT = 2.5
BORON_TOTAL = 416.0
AIR_CARBON = 14.0
START_HYDROGEN = 2.0
ROW_DIFFUSION = 0.1


def padded(cells, sides, width):
    for axis, dim in sides:
        count = lax.axis_size(axis)
        head = lax.slice_in_dim(cells, 0, width, axis=dim)
        tail = lax.slice_in_dim(cells, cells.shape[dim] - width, cells.shape[dim], axis=dim)
        cells = jnp.concatenate(
            [
                lax.ppermute(tail, axis, [(i, (i + 1) % count) for i in range(count)]),
                cells,
                lax.ppermute(head, axis, [((i + 1) % count, i) for i in range(count)]),
            ],
            axis=dim,
        )
    return cells


def spread(value, axis, source):
    kept = jnp.where(lax.axis_index(axis) == source, value, 0).astype(value.dtype)
    return lax.psum(kept, axis)


def chemistry(carbon, alkalinity, piston, surface_sea):
    hydrogen = jnp.full_like(carbon, START_HYDROGEN)
    for iteration in range(NEWTON):
        square = hydrogen * hydrogen
        denominator = square + DISSOCIATION_ONE * hydrogen + DISSOCIATION_ONE * DISSOCIATION_TWO
        carbonate = carbon * DISSOCIATION_ONE * (hydrogen + 2.0 * DISSOCIATION_TWO) / denominator
        borate = BORON_TOTAL * BORATE_CONSTANT / (hydrogen + BORATE_CONSTANT)
        derivative = -carbon * DISSOCIATION_ONE * (
            square + 4.0 * DISSOCIATION_TWO * hydrogen + DISSOCIATION_ONE * DISSOCIATION_TWO
        ) / (denominator * denominator) - borate / (hydrogen + BORATE_CONSTANT)
        hydrogen = hydrogen - (carbonate + borate - alkalinity) / derivative
    square = hydrogen * hydrogen
    denominator = square + DISSOCIATION_ONE * hydrogen + DISSOCIATION_ONE * DISSOCIATION_TWO
    dissolved = carbon * square / denominator
    return surface_sea * piston * (AIR_CARBON - dissolved)


def forward_shift(source, offset):
    padding = jnp.zeros(source.shape[:-1] + (offset,), source.dtype)
    return jnp.concatenate([source[..., offset:], padding], axis=-1)


def backward_shift(source, offset):
    padding = jnp.zeros(source.shape[:-1] + (offset,), source.dtype)
    return jnp.concatenate([padding, source[..., :-offset]], axis=-1)


def column_weights(sea_float, mixing):
    cell_index = jnp.arange(LEVELS * ROWS, dtype=jnp.int32)
    row_open = (cell_index % ROWS < ROWS - 1).astype(jnp.float32)
    level_open = (cell_index // ROWS < LEVELS - 1).astype(jnp.float32)
    row_weight = ROW_DIFFUSION * row_open * sea_float * forward_shift(sea_float, 1)
    level_weight = mixing * level_open * sea_float * forward_shift(sea_float, ROWS)
    return (row_weight, level_weight)


def column_mix(source, row_weight, level_weight):
    row_flux = row_weight * (forward_shift(source, 1) - source)
    level_flux = level_weight * (forward_shift(source, ROWS) - source)
    return row_flux - backward_shift(row_flux, 1) + level_flux - backward_shift(level_flux, ROWS)


def zonal_weights(sea_float, sea_east, velocity):
    opened = sea_float * sea_east
    magnitude = jnp.abs(velocity)
    return jnp.stack(
        [
            opened * (-velocity - magnitude) / 12.0,
            opened * (7.0 * velocity + 3.0 * magnitude) / 12.0,
            opened * (7.0 * velocity - 3.0 * magnitude) / 12.0,
            opened * (magnitude - velocity) / 12.0,
        ]
    )


def trim_rim(source, keep_rim, outer_rim, dimension):
    length = source.shape[dimension] - 2 * outer_rim
    return lax.slice_in_dim(
        source, outer_rim - keep_rim, outer_rim + length + keep_rim, axis=dimension
    )


def surface_slopes(carbon, alkalinity, piston, surface_sea):

    def uptake_of(carbon_in, alkalinity_in):
        return chemistry(carbon_in, alkalinity_in, piston, surface_sea)

    uptake, pullback = jax.vjp(uptake_of, carbon, alkalinity)
    by_carbon, by_alkalinity = pullback(jnp.ones_like(carbon))
    return (uptake, jnp.stack([by_carbon, by_alkalinity]))


def advance_rim(extended, weights, row_weight, level_weight, uptake):
    length = extended.shape[1]
    face_flux = (
        weights[0, 1 : length - 2] * extended[:, 0 : length - 3]
        + weights[1, 1 : length - 2] * extended[:, 1 : length - 2]
        + weights[2, 1 : length - 2] * extended[:, 2 : length - 1]
        + weights[3, 1 : length - 2] * extended[:, 3:length]
    )
    interior = extended[:, 2 : length - 2]
    zonal_term = -(face_flux[:, 1:] - face_flux[:, :-1])
    transported = interior + zonal_term + column_mix(interior, row_weight, level_weight)
    surface_row = transported[0, :, :ROWS] + uptake
    carbon = jnp.concatenate([surface_row, transported[0, :, ROWS:]], axis=-1)
    return jnp.stack([carbon, transported[1]])


def retreat(extended, weights, row_weight, level_weight, slopes, objective_seeds):
    length = extended.shape[2]
    difference = extended[:, :, 1:] - extended[:, :, :-1]
    zonal_term = (
        weights[0, 3 : length - 1] * difference[:, :, 3 : length - 1]
        + weights[1, 2 : length - 2] * difference[:, :, 2 : length - 2]
        + weights[2, 1 : length - 3] * difference[:, :, 1 : length - 3]
        + weights[3, 0 : length - 4] * difference[:, :, 0 : length - 4]
    )
    interior = extended[:, :, 2 : length - 2]
    adjoint = interior + zonal_term + column_mix(interior, row_weight, level_weight)
    forcing = interior[:, 0, :, :ROWS] + objective_seeds
    surface = adjoint[..., :ROWS] + slopes[None] * forcing[:, None]
    return jnp.concatenate([surface, adjoint[..., ROWS:]], axis=-1)


def body(
    adjoint_in, checkpoint_store, interval, sea_mask, zonal_speed, mixing, piston, cell_area, region
):
    groups = adjoint_in.shape[0]
    cell_count = adjoint_in.shape[3]
    rim_depth = 4
    statics = jnp.concatenate(
        [
            sea_mask.astype(jnp.float32),
            zonal_speed,
            mixing,
            piston,
            cell_area,
            region.astype(jnp.float32),
        ],
        axis=1,
    )
    widened = padded(statics, (("tile", 0),), rim_depth)
    sea_wide = widened[:, :cell_count]
    speed_wide = widened[:, cell_count : 2 * cell_count]
    mixing_wide = widened[:, 2 * cell_count : 3 * cell_count]
    offset = 3 * cell_count
    piston_wide = widened[:, offset : offset + ROWS]
    area_wide = widened[:, offset + ROWS : offset + 2 * ROWS]
    region_wide = widened[:, offset + 2 * ROWS : offset + 3 * ROWS]
    sea_east = jnp.concatenate([sea_wide[1:], jnp.zeros_like(sea_wide[:1])], axis=0)
    weights = zonal_weights(sea_wide, sea_east, speed_wide)
    row_weight, level_weight = column_weights(sea_wide, mixing_wide)
    surface_sea = sea_wide[:, :ROWS]
    targets = (lax.axis_index("obj") * groups + jnp.arange(groups, dtype=jnp.int32)).astype(
        jnp.float32
    )
    objective_seeds = area_wide[None] * (region_wide[None] == targets[:, None, None]).astype(
        jnp.float32
    )
    owners = lax.axis_size("obj")
    owner_index = interval[0] % owners
    band = 2 * ROWS
    stored = lax.dynamic_index_in_dim(checkpoint_store, interval[0] // owners, 0, keepdims=False)
    stored = spread(stored[:, :, :band], "obj", owner_index)
    initial_wide = padded(stored, (("tile", 1),), rim_depth)
    inner_rim = 2
    piston_inner = trim_rim(piston_wide, inner_rim, rim_depth, 0)
    sea_inner = trim_rim(surface_sea, inner_rim, rim_depth, 0)
    initial_inner = trim_rim(initial_wide, inner_rim, rim_depth, 1)
    uptake_first, slopes_first = surface_slopes(
        initial_inner[0, :, :ROWS], initial_inner[1, :, :ROWS], piston_inner, sea_inner
    )
    following = advance_rim(
        initial_wide,
        weights[:, :, :band],
        trim_rim(row_weight, inner_rim, rim_depth, 0)[:, :band],
        trim_rim(level_weight, inner_rim, rim_depth, 0)[:, :band],
        uptake_first,
    )
    _, slopes_second = surface_slopes(
        following[0, :, :ROWS], following[1, :, :ROWS], piston_inner, sea_inner
    )
    extended = padded(adjoint_in, (("tile", 2),), rim_depth)
    middle = retreat(
        extended,
        weights,
        trim_rim(row_weight, inner_rim, rim_depth, 0),
        trim_rim(level_weight, inner_rim, rim_depth, 0),
        slopes_second,
        trim_rim(objective_seeds, inner_rim, rim_depth, 1),
    )
    return retreat(
        middle,
        trim_rim(weights, inner_rim, rim_depth, 1),
        trim_rim(row_weight, 0, rim_depth, 0),
        trim_rim(level_weight, 0, rim_depth, 0),
        trim_rim(slopes_first, 0, inner_rim, 1),
        trim_rim(objective_seeds, 0, rim_depth, 1),
    )


def solution(mesh):
    placed = (
        P("obj", None, "tile", None),
        P("obj", None, "tile", None),
        P(),
        P("tile", None),
        P("tile", None),
        P("tile", None),
        P("tile", None),
        P("tile", None),
        P("tile", None),
    )
    return jax.shard_map(
        body, mesh=mesh, in_specs=placed, out_specs=P("obj", None, "tile", None), check_vma=False
    )
```

profile of v0, /device:TPU:1, one launch (start us, length us, event | category | flops | bytes accessed | tf_op | source)
XLA Modules:
  0.0 127.1 jit_solution(1453807047856551090)
XLA Ops:
  0.7 0.3 copy-done
  1.1 65.3 %psum.7 = f32[2,16,64]{2,1,0:T(8,128)S(1)} all-reduce(f32[2,16,64]{2,1,0:T(8,128)S(1)} %slice_select_fusion), channel_id=1, replica_groups=mesh['tile'=16,'obj'=16] {'obj'}, use_global_device_ids=true, to_apply=%region_0.1 | all-reduce | flops 2048 | bytes 16384 | tf_op jit(solution)/shard_map/psum | solution.py:36
  66.3 0.3 collective-permute-start.4
  66.7 5.3 %collective-permute-start.5 = (f32[2,4,64]{2,1,0:T(4,128)S(1)}, f32[2,4,64]{2,1,0:T(4,128)S(1)}, u32[]{:S(2)}, u32[]{:S(2)}) collective-permute-start(f32[2,4,64]{2,1,0:T(4,128)S(1)} %get-tuple-element.44), channel_id=1, source_target_pairs={{16,0},{32,16},{48,32},{64,48},{80,64},{96,80},{112,96},{128,112},... | collective-permute-start | bytes 6152 | tf_op jit(solution)/shard_map/ppermute | solution.py:27
  72.0 0.7 convert_element_type.25
  72.7 0.8 convert_element_type.24
  73.5 1.0 concatenate.67
  74.6 3.6 %collective-permute-start.3 = (f32[4,3168]{1,0:T(4,128)S(1)}, f32[4,3168]{1,0:T(4,128)S(1)}, u32[]{:S(2)}, u32[]{:S(2)}) collective-permute-start(f32[4,3168]{1,0:T(4,128)S(1)} %get-tuple-element.38), channel_id=1, source_target_pairs={{16,0},{32,16},{48,32},{64,48},{80,64},{96,80},{112,96},{128,112},... | collective-permute-start | bytes 152072 | tf_op jit(solution)/shard_map/ppermute | solution.py:27
  78.1 1.8 %fusion.65 = (f32[16,2,4,1024]{3,2,0,1:T(4,128)S(1)}, f32[16,2,4,1024]{3,2,0,1:T(4,128)S(1)}) fusion(f32[16,2,16,1024]{3,2,1,0:T(8,128)} %param.9), kind=kLoop, calls=%fused_computation.232 | loop fusion | bytes 2097152 | tf_op jit(solution)/shard_map/slice | solution.py:22
  80.1 3.6 %collective-permute-start.1 = (f32[16,2,4,1024]{3,2,0,1:T(4,128)S(1)}, f32[16,2,4,1024]{3,2,0,1:T(4,128)S(1)}, u32[]{:S(2)}, u32[]{:S(2)}) collective-permute-start(f32[16,2,4,1024]{3,2,0,1:T(4,128)S(1)} %get-tuple-element.29), channel_id=1, source_target_pairs={{16,0},{32,16},{48,32},{64,48},{80,64},{96,80},{112,96},{128,112},... | collective-permute-start | bytes 1572872 | tf_op jit(solution)/shard_map/ppermute | solution.py:27
  84.2 0.7 slice_bitcast_fusion.7
  84.9 0.7 slice_bitcast_fusion.5
  85.8 0.2 add_bitcast_fusion.1
  86.6 0.6 slice.448
  87.2 0.6 slice.450
  87.9 0.7 slice_bitcast_fusion.3
  88.5 0.7 slice_bitcast_fusion.1
  89.2 13.3 %collective-permute-done = f32[16,2,4,1024]{3,2,0,1:T(4,128)S(1)} collective-permute-done((f32[16,2,4,1024]{3,2,0,1:T(4,128)S(1)}, f32[16,2,4,1024]{3,2,0,1:T(4,128)S(1)}, u32[]{:S(2)}, u32[]{:S(2)}) %collective-permute-start) | collective-permute-done | bytes 524320 | tf_op jit(solution)/shard_map/ppermute | solution.py:25
  102.5 2.1 %collective-permute-done.1 = f32[16,2,4,1024]{3,2,0,1:T(4,128)S(1)} collective-permute-done((f32[16,2,4,1024]{3,2,0,1:T(4,128)S(1)}, f32[16,2,4,1024]{3,2,0,1:T(4,128)S(1)}, u32[]{:S(2)}, u32[]{:S(2)}) %collective-permute-start.1) | collective-permute-done | bytes 524320 | tf_op jit(solution)/shard_map/ppermute | solution.py:27
  104.7 0.5 pad_maximum_fusion
  105.2 1.2 slice.398
  106.4 0.5 slice_subtract_fusion
  106.9 2.9 %slice.403 = f32[16,2,20,992]{3,2,0,1:T(8,128)} slice(f32[16,2,24,1024]{3,2,0,1:T(8,128)S(1)} %pad_maximum_fusion), slice={[0:16], [0:2], [2:22], [32:1024]} | slice | bytes 5079040 | tf_op jit(solution)/shard_map/slice | solution.py:58
  109.8 4.3 %fusion.4 = (f32[16,2,20,1024]{3,2,0,1:T(8,128)S(1)}, f32[16,2,20,1024]{3,2,0,1:T(8,128)S(1)}, f32[16,2,20,1024]{3,2,0,1:T(8,128)S(1)}) fusion(f32[16,2,23,1024]{3,2,0,1:T(8,128)S(1)} %slice_subtract_fusion, f32[16,2,24,1024]{3,2,0,1:T(8,128)S(1)} %pad_maximum_fusion, f32[20,1024]{1,0:T(8,128)S(1)} %copy-done.3, f32[20,1024]{1,0:T(8,128)S(1)} %copy-done.4, ...), kind=kLoop, calls=%fused_computation.8 | loop fusion | flops 7864320 | bytes 26621440 | tf_op jit(solution)/shard_map/add | solution.py:137
  114.1 2.4 %copy_add_fusion = f32[16,2,20,1024]{3,2,1,0:T(8,128)S(1)} fusion(f32[16,2,20,1024]{3,2,0,1:T(8,128)S(1)} %get-tuple-element.25, f32[16,2,20,992]{3,2,0,1:T(8,128)S(1)} %bitcast.356, f32[16,2,20,1024]{3,2,0,1:T(8,128)S(1)} %get-tuple-element.27, f32[16,2,20,1024]{3,2,0,1:T(8,128)S(1)} %get-tuple-element.26, f32[16,2,20,1023]{3,2,0,1:T(8,128)S(1)} %bitcast.355), kind=kLoop, calls=%fused_computation.16 | loop fusion | flops 2621440 | bytes 15644160 | tf_op jit(solution)/shard_map/add | solution.py:137
  116.5 0.8 slice.451
  117.3 0.9 slice.433
  118.4 1.7 %fusion.1 = f32[16,2,19,1024]{3,2,1,0:T(8,128)S(1)} fusion(f32[16,2,20,32]{3,2,1,0:T(8,128)S(1)} %slice_add_fusion, f32[16,2,20,992]{3,2,1,0:T(8,128)S(1)} %slice.433), kind=kLoop, calls=%fused_computation.4 | loop fusion | flops 1867776 | bytes 5111808 | tf_op jit(solution)/shard_map/sub | solution.py:129
  120.2 1.9 %fusion.9 = (f32[16,2,16,1024]{3,2,1,0:T(8,128)S(1)}, f32[16,2,16,1024]{3,2,1,0:T(8,128)S(1)}) fusion(f32[16,2,20,992]{3,2,1,0:T(8,128)S(1)} %slice.433, f32[16,2,20,32]{3,2,1,0:T(8,128)S(1)} %slice_add_fusion, f32[16,1024]{1,0:T(8,128)S(1)} %copy-done.5, f32[16,2,16,992]{3,2,1,0:T(8,128)S(1)} %slice.451, f32[16,1024]{1,0:T(8,128)S(1)} %copy-done.6), kind=kLoop, calls=%fused_computation.24 | loop fusion | flops 5242880 | bytes 8978432 | tf_op jit(solution)/shard_map/mul | solution.py:76
  122.1 2.4 %fusion.12 = f32[16,2,16,1024]{3,2,1,0:T(8,128)S(1)} fusion(f32[16,2,19,1024]{3,2,1,0:T(8,128)S(1)} %fusion.1, f32[16,2,16,992]{3,2,1,0:T(8,128)S(1)} %bitcast.358, f32[16,2,16,1024]{3,2,1,0:T(8,128)S(1)} %get-tuple-element.24, f32[16,2,16,1024]{3,2,1,0:T(8,128)S(1)} %get-tuple-element.23, f32[16,2,16,1023]{3,2,1,0:T(8,128)S(1)} %bitcast.357, ...), kind=kLoop, calls=%fused_computation.29 | loop fusion | flops 6815744 | bytes 21690368 | tf_op jit(solution)/shard_map/add | solution.py:137
  124.6 0.6 slice.456
  125.2 1.9 %pad_maximum_fusion.1 = f32[16,2,16,1024]{3,2,1,0:T(8,128)} fusion(f32[16,2,16,992]{3,2,1,0:T(8,128)S(1)} %slice.456, f32[16,2,16,32]{3,2,1,0:T(8,128)S(1)} %slice_add_fusion.1), kind=kLoop, calls=%fused_computation.35 | loop fusion | flops 524288 | bytes 4194304 | tf_op jit(solution)/shard_map/concatenate | solution.py:140
  (65 shorter events, 1.8 us)
Async XLA Ops:
  0.0 1.1 copy-start
  66.3 13.7 %collective-permute-start.4 = (f32[2,4,64]{2,1,0:T(4,128)S(1)}, f32[2,4,64]{2,1,0:T(4,128)S(1)}, u32[]{:S(2)}, u32[]{:S(2)}) collective-permute-start(f32[2,4,64]{2,1,0:T(4,128)S(1)} %get-tuple-element.43), channel_id=1, source_target_pairs={{0,16},{16,32},{32,48},{48,64},{64,80},{80,96},{96,112},{112,128},... | collective-permute-start | bytes 6152 | tf_op jit(solution)/shard_map/ppermute | solution.py:25
  66.7 17.0 %collective-permute-start.5 = (f32[2,4,64]{2,1,0:T(4,128)S(1)}, f32[2,4,64]{2,1,0:T(4,128)S(1)}, u32[]{:S(2)}, u32[]{:S(2)}) collective-permute-start(f32[2,4,64]{2,1,0:T(4,128)S(1)} %get-tuple-element.44), channel_id=1, source_target_pairs={{16,0},{32,16},{48,32},{64,48},{80,64},{96,80},{112,96},{128,112},... | collective-permute-start | bytes 6152 | tf_op jit(solution)/shard_map/ppermute | solution.py:27
  74.5 9.4 %collective-permute-start.2 = (f32[4,3168]{1,0:T(4,128)S(1)}, f32[4,3168]{1,0:T(4,128)S(1)}, u32[]{:S(2)}, u32[]{:S(2)}) collective-permute-start(f32[4,3168]{1,0:T(4,128)S(1)} %get-tuple-element.37), channel_id=1, source_target_pairs={{0,16},{16,32},{32,48},{48,64},{64,80},{80,96},{96,112},{112,128},... | collective-permute-start | bytes 152072 | tf_op jit(solution)/shard_map/ppermute | solution.py:25
  74.6 9.3 %collective-permute-start.3 = (f32[4,3168]{1,0:T(4,128)S(1)}, f32[4,3168]{1,0:T(4,128)S(1)}, u32[]{:S(2)}, u32[]{:S(2)}) collective-permute-start(f32[4,3168]{1,0:T(4,128)S(1)} %get-tuple-element.38), channel_id=1, source_target_pairs={{16,0},{32,16},{48,32},{64,48},{80,64},{96,80},{112,96},{128,112},... | collective-permute-start | bytes 152072 | tf_op jit(solution)/shard_map/ppermute | solution.py:27
  79.9 22.6 %collective-permute-start = (f32[16,2,4,1024]{3,2,0,1:T(4,128)S(1)}, f32[16,2,4,1024]{3,2,0,1:T(4,128)S(1)}, u32[]{:S(2)}, u32[]{:S(2)}) collective-permute-start(f32[16,2,4,1024]{3,2,0,1:T(4,128)S(1)} %get-tuple-element.28), channel_id=1, source_target_pairs={{0,16},{16,32},{32,48},{48,64},{64,80},{80,96},{96,112},{112,128},... | collective-permute-start | bytes 1572872 | tf_op jit(solution)/shard_map/ppermute | solution.py:25
  80.1 24.6 %collective-permute-start.1 = (f32[16,2,4,1024]{3,2,0,1:T(4,128)S(1)}, f32[16,2,4,1024]{3,2,0,1:T(4,128)S(1)}, u32[]{:S(2)}, u32[]{:S(2)}) collective-permute-start(f32[16,2,4,1024]{3,2,0,1:T(4,128)S(1)} %get-tuple-element.29), channel_id=1, source_target_pairs={{16,0},{32,16},{48,32},{64,48},{80,64},{96,80},{112,96},{128,112},... | collective-permute-start | bytes 1572872 | tf_op jit(solution)/shard_map/ppermute | solution.py:27
  84.0 20.7 %copy-start.1 = (f32[16,2,16,1024]{3,2,1,0:T(8,128)S(1)}, f32[16,2,16,1024]{3,2,1,0:T(8,128)}, u32[]{:S(2)}) copy-start(f32[16,2,16,1024]{3,2,1,0:T(8,128)} %param.9) | copy-start | bytes 6291460
  106.9 2.9 %copy-start.2 = (f32[20,1024]{1,0:T(8,128)S(1)}, f32[20,1024]{1,0:T(8,128)}, u32[]{:S(2)}) copy-start(f32[20,1024]{1,0:T(8,128)} %get-tuple-element.52) | copy-start | bytes 245764
  106.9 2.9 %copy-start.3 = (f32[20,1024]{1,0:T(8,128)S(1)}, f32[20,1024]{1,0:T(8,128)}, u32[]{:S(2)}) copy-start(f32[20,1024]{1,0:T(8,128)} %get-tuple-element.45) | copy-start | bytes 245764
  106.9 2.9 %copy-start.4 = (f32[20,1024]{1,0:T(8,128)S(1)}, f32[20,1024]{1,0:T(8,128)}, u32[]{:S(2)}) copy-start(f32[20,1024]{1,0:T(8,128)} %get-tuple-element.46) | copy-start | bytes 245764
  118.3 1.8 %copy-start.5 = (f32[16,1024]{1,0:T(8,128)S(1)}, f32[16,1024]{1,0:T(8,128)}, u32[]{:S(2)}) copy-start(f32[16,1024]{1,0:T(8,128)} %slice.448) | copy-start | bytes 196612
  118.4 1.8 %copy-start.6 = (f32[16,1024]{1,0:T(8,128)S(1)}, f32[16,1024]{1,0:T(8,128)}, u32[]{:S(2)}) copy-start(f32[16,1024]{1,0:T(8,128)} %slice.450) | copy-start | bytes 196612
  120.1 1.9 %copy-start.7 = (f32[16,1024]{1,0:T(8,128)S(1)}, f32[16,1024]{1,0:T(8,128)}, u32[]{:S(2)}) copy-start(f32[16,1024]{1,0:T(8,128)} %get-tuple-element.55) | copy-start | bytes 196612
  120.1 1.9 %copy-start.8 = (f32[16,1024]{1,0:T(8,128)S(1)}, f32[16,1024]{1,0:T(8,128)}, u32[]{:S(2)}) copy-start(f32[16,1024]{1,0:T(8,128)} %get-tuple-element.56) | copy-start | bytes 196612
  120.2 1.9 %copy-start.9 = (f32[16,1024]{1,0:T(8,128)S(1)}, f32[16,1024]{1,0:T(8,128)}, u32[]{:S(2)}) copy-start(f32[16,1024]{1,0:T(8,128)} %get-tuple-element.47) | copy-start | bytes 196612
  120.2 1.9 %copy-start.10 = (f32[16,1024]{1,0:T(8,128)S(1)}, f32[16,1024]{1,0:T(8,128)}, u32[]{:S(2)}) copy-start(f32[16,1024]{1,0:T(8,128)} %get-tuple-element.48) | copy-start | bytes 196612
where the time goes:
time: 127 us
  blocking collectives  65.3 us (51%)
  other arithmetic  18.5 us (15%)
  waiting for transfers between devices  15.4 us (12%)
  local copies, waits for them, and re-layouts  13.8 us (11%)
  starting transfers between devices  12.9 us (10%)
    psum x1, blocking collectives, spread(): return lax.psum(kept, axis)  65.3 us
    ppermute x3, waiting for transfers between devices, padded(): lax.ppermute(tail, axis, [(i, (i + 1) % count) for i in range(count)])  13.3 us
    ppermute x3, starting transfers between devices, padded(): lax.ppermute(head, axis, [((i + 1) % count, i) for i in range(count)])  12.5 us
    add x3, other arithmetic, retreat(): interior + zonal_term + column_mix(interior, row_weight, level_weight)  9.16 us
    slice x7, local copies, waits for them, and re-layouts, forward_shift(): return jnp.concatenate([source[..., offset:], padding], axis=-1)  5.15 us
  transfers between devices with their start and end apart: 6, of which 2 were waited for; matrix products, arithmetic and copies ran while one was open for 8% of the time, Pallas kernels for 0%

commit v1 on v0

--- a/solution.py
+++ b/solution.py
@@ -33,7 +33,7 @@
 
 def spread(value, axis, source):
     kept = jnp.where(lax.axis_index(axis) == source, value, 0).astype(value.dtype)
-    return lax.psum(kept, axis)
+    return jnp.sum(lax.all_gather(kept, axis), axis=0)
 
 
 def chemistry(carbon, alkalinity, piston, surface_sea):

time: 127 us -> 88.8 us (0.70)
  blocking collectives: 65.3 us -> 25.6 us
  starting transfers between devices: 12.9 us -> 14.8 us
    psum x1 -> x0, blocking collectives: 65.3 us -> none  [spread(): return lax.psum(kept, axis)]
    all_gather x0 -> x1, blocking collectives: none -> 25.6 us  [spread(): return jnp.sum(lax.all_gather(kept, axis), axis=0)]
    ppermute x3, starting transfers between devices: 0.48 us -> 2.27 us  [padded(): lax.ppermute(tail, axis, [(i, (i + 1) % count) for i in range(count)])]
where the time goes in v1:
time: 88.8 us; the launch traced here: 88.6 us
  blocking collectives  25.6 us (29%)
  other arithmetic  18.6 us (21%)
  waiting for transfers between devices  14.9 us (17%)
  starting transfers between devices  14.8 us (17%)
  local copies, waits for them, and re-layouts  13.5 us (15%)
  between operations  1.12 us (1%)
    all_gather x1, blocking collectives, spread(): return jnp.sum(lax.all_gather(kept, axis), axis=0)  25.6 us
    ppermute x3, waiting for transfers between devices, padded(): lax.ppermute(tail, axis, [(i, (i + 1) % count) for i in range(count)])  12.7 us
    ppermute x3, starting transfers between devices, padded(): lax.ppermute(head, axis, [((i + 1) % count, i) for i in range(count)])  12.6 us
    add x3, other arithmetic, retreat(): interior + zonal_term + column_mix(interior, row_weight, level_weight)  9.16 us
    slice x7, local copies, waits for them, and re-layouts, forward_shift(): return jnp.concatenate([source[..., offset:], padding], axis=-1)  5.15 us
    ppermute x3, starting transfers between devices, padded(): lax.ppermute(tail, axis, [(i, (i + 1) % count) for i in range(count)])  2.27 us
    sub x2, other arithmetic, retreat(): difference = extended[:, :, 1:] - extended[:, :, :-1]  2.24 us
    ppermute x3, waiting for transfers between devices, padded(): lax.ppermute(head, axis, [((i + 1) % count, i) for i in range(count)])  2.23 us
  transfers between devices with their start and end apart: 6, of which 2 were waited for; matrix products, arithmetic and copies ran while one was open for 8% of the time, Pallas kernels for 0%

profile of v1, /device:TPU:1, one launch (start us, length us, event | category | flops | bytes accessed | tf_op | source)
XLA Modules:
  0.0 88.6 jit_solution(17942203938662435904)
XLA Ops:
  0.0 0.8 convert_element_type.25
  0.8 0.8 convert_element_type.24
  1.6 1.0 %concatenate.67 = f32[16,3168]{1,0:T(8,128)S(1)} concatenate(f32[16,1024]{1,0:T(8,128)S(1)} %convert_element_type.24, f32[16,1024]{1,0:T(8,128)} %param.13, f32[16,1024]{1,0:T(8,128)} %param.14, f32[16,32]{1,0:T(8,128)} %param.15, f32[16,32]{1,0:T(8,128)} %param.16, f32[16,32]{1,0:T(8,128)S(1)} %convert_element_type.25), dimensions={1} | concatenate | bytes 405504 | tf_op jit(solution)/shard_map/concatenate | solution.py:149
  2.6 2.1 %collective-permute-start.2 = (f32[4,3168]{1,0:T(4,128)S(1)}, f32[4,3168]{1,0:T(4,128)S(1)}, u32[]{:S(2)}, u32[]{:S(2)}) collective-permute-start(f32[4,3168]{1,0:T(4,128)S(1)} %get-tuple-element.37), channel_id=1, source_target_pairs={{0,16},{16,32},{32,48},{48,64},{64,80},{80,96},{96,112},{112,128},... | collective-permute-start | bytes 152072 | tf_op jit(solution)/shard_map/ppermute | solution.py:25
  4.7 5.4 %collective-permute-start.3 = (f32[4,3168]{1,0:T(4,128)S(1)}, f32[4,3168]{1,0:T(4,128)S(1)}, u32[]{:S(2)}, u32[]{:S(2)}) collective-permute-start(f32[4,3168]{1,0:T(4,128)S(1)} %get-tuple-element.38), channel_id=1, source_target_pairs={{16,0},{32,16},{48,32},{64,48},{80,64},{96,80},{112,96},{128,112},... | collective-permute-start | bytes 152072 | tf_op jit(solution)/shard_map/ppermute | solution.py:27
  10.8 25.6 %all-gather = f32[32,16,64]{2,1,0:T(8,128)S(1)} all-gather(f32[2,16,64]{2,1,0:T(8,128)S(1)} %slice_select_fusion), channel_id=2, replica_groups=mesh['tile'=16,'obj'=16] {'obj'}, dimensions={0}, use_global_device_ids=true | all-gather | bytes 139264 | tf_op jit(solution)/shard_map/all_gather | solution.py:36
  36.6 3.6 %collective-permute-start.5 = (f32[2,4,64]{2,1,0:T(4,128)S(1)}, f32[2,4,64]{2,1,0:T(4,128)S(1)}, u32[]{:S(2)}, u32[]{:S(2)}) collective-permute-start(f32[2,4,64]{2,1,0:T(4,128)S(1)} %get-tuple-element.44), channel_id=1, source_target_pairs={{16,0},{32,16},{48,32},{64,48},{80,64},{96,80},{112,96},{128,112},... | collective-permute-start | bytes 6152 | tf_op jit(solution)/shard_map/ppermute | solution.py:27
  40.1 1.8 %fusion.65 = (f32[16,2,4,1024]{3,2,0,1:T(4,128)S(1)}, f32[16,2,4,1024]{3,2,0,1:T(4,128)S(1)}) fusion(f32[16,2,16,1024]{3,2,1,0:T(8,128)} %param.9), kind=kLoop, calls=%fused_computation.232 | loop fusion | bytes 2097152 | tf_op jit(solution)/shard_map/slice | solution.py:22
  42.0 3.6 %collective-permute-start.1 = (f32[16,2,4,1024]{3,2,0,1:T(4,128)S(1)}, f32[16,2,4,1024]{3,2,0,1:T(4,128)S(1)}, u32[]{:S(2)}, u32[]{:S(2)}) collective-permute-start(f32[16,2,4,1024]{3,2,0,1:T(4,128)S(1)} %get-tuple-element.29), channel_id=1, source_target_pairs={{16,0},{32,16},{48,32},{64,48},{80,64},{96,80},{112,96},{128,112},... | collective-permute-start | bytes 1572872 | tf_op jit(solution)/shard_map/ppermute | solution.py:27
  46.2 0.7 slice_bitcast_fusion.7
  46.9 0.7 slice_bitcast_fusion.5
  47.8 0.2 add_bitcast_fusion.1
  48.1 0.2 add_bitcast_fusion.3
  48.6 0.6 slice.448
  49.2 0.6 slice.450
  49.9 0.7 slice_bitcast_fusion.3
  50.5 0.7 slice_bitcast_fusion.1
  51.2 12.7 %collective-permute-done = f32[16,2,4,1024]{3,2,0,1:T(4,128)S(1)} collective-permute-done((f32[16,2,4,1024]{3,2,0,1:T(4,128)S(1)}, f32[16,2,4,1024]{3,2,0,1:T(4,128)S(1)}, u32[]{:S(2)}, u32[]{:S(2)}) %collective-permute-start) | collective-permute-done | bytes 524320 | tf_op jit(solution)/shard_map/ppermute | solution.py:25
  63.9 2.2 %collective-permute-done.1 = f32[16,2,4,1024]{3,2,0,1:T(4,128)S(1)} collective-permute-done((f32[16,2,4,1024]{3,2,0,1:T(4,128)S(1)}, f32[16,2,4,1024]{3,2,0,1:T(4,128)S(1)}, u32[]{:S(2)}, u32[]{:S(2)}) %collective-permute-start.1) | collective-permute-done | bytes 524320 | tf_op jit(solution)/shard_map/ppermute | solution.py:27
  66.1 0.5 pad_maximum_fusion
  66.6 1.2 %slice.398 = f32[16,2,20,1023]{3,2,0,1:T(8,128)S(1)} slice(f32[16,2,24,1024]{3,2,0,1:T(8,128)S(1)} %pad_maximum_fusion), slice={[0:16], [0:2], [2:22], [1:1024]} | slice | bytes 5237760 | tf_op jit(solution)/shard_map/slice | solution.py:58
  67.8 0.5 slice_subtract_fusion
  68.4 2.9 %slice.403 = f32[16,2,20,992]{3,2,0,1:T(8,128)} slice(f32[16,2,24,1024]{3,2,0,1:T(8,128)S(1)} %pad_maximum_fusion), slice={[0:16], [0:2], [2:22], [32:1024]} | slice | bytes 5079040 | tf_op jit(solution)/shard_map/slice | solution.py:58
  71.3 4.3 %fusion.4 = (f32[16,2,20,1024]{3,2,0,1:T(8,128)S(1)}, f32[16,2,20,1024]{3,2,0,1:T(8,128)S(1)}, f32[16,2,20,1024]{3,2,0,1:T(8,128)S(1)}) fusion(f32[16,2,23,1024]{3,2,0,1:T(8,128)S(1)} %slice_subtract_fusion, f32[16,2,24,1024]{3,2,0,1:T(8,128)S(1)} %pad_maximum_fusion, f32[20,1024]{1,0:T(8,128)S(1)} %copy-done.3, f32[20,1024]{1,0:T(8,128)S(1)} %copy-done.4, ...), kind=kLoop, calls=%fused_computation.8 | loop fusion | flops 7864320 | bytes 26621440 | tf_op jit(solution)/shard_map/add | solution.py:137
  75.6 2.4 %copy_add_fusion = f32[16,2,20,1024]{3,2,1,0:T(8,128)S(1)} fusion(f32[16,2,20,1024]{3,2,0,1:T(8,128)S(1)} %get-tuple-element.25, f32[16,2,20,992]{3,2,0,1:T(8,128)S(1)} %bitcast.357, f32[16,2,20,1024]{3,2,0,1:T(8,128)S(1)} %get-tuple-element.27, f32[16,2,20,1024]{3,2,0,1:T(8,128)S(1)} %get-tuple-element.26, f32[16,2,20,1023]{3,2,0,1:T(8,128)S(1)} %bitcast.356), kind=kLoop, calls=%fused_computation.16 | loop fusion | flops 2621440 | bytes 15644160 | tf_op jit(solution)/shard_map/add | solution.py:137
  78.0 0.8 slice.451
  78.8 0.9 slice.433
  79.8 1.7 %fusion.1 = f32[16,2,19,1024]{3,2,1,0:T(8,128)S(1)} fusion(f32[16,2,20,32]{3,2,1,0:T(8,128)S(1)} %slice_add_fusion, f32[16,2,20,992]{3,2,1,0:T(8,128)S(1)} %slice.433), kind=kLoop, calls=%fused_computation.4 | loop fusion | flops 1867776 | bytes 5111808 | tf_op jit(solution)/shard_map/sub | solution.py:129
  81.6 1.9 %fusion.9 = (f32[16,2,16,1024]{3,2,1,0:T(8,128)S(1)}, f32[16,2,16,1024]{3,2,1,0:T(8,128)S(1)}) fusion(f32[16,2,20,992]{3,2,1,0:T(8,128)S(1)} %slice.433, f32[16,2,20,32]{3,2,1,0:T(8,128)S(1)} %slice_add_fusion, f32[16,1024]{1,0:T(8,128)S(1)} %copy-done.5, f32[16,2,16,992]{3,2,1,0:T(8,128)S(1)} %slice.451, f32[16,1024]{1,0:T(8,128)S(1)} %copy-done.6), kind=kLoop, calls=%fused_computation.24 | loop fusion | flops 5242880 | bytes 8978432 | tf_op jit(solution)/shard_map/mul | solution.py:76
  83.6 2.4 %fusion.12 = f32[16,2,16,1024]{3,2,1,0:T(8,128)S(1)} fusion(f32[16,2,19,1024]{3,2,1,0:T(8,128)S(1)} %fusion.1, f32[16,2,16,992]{3,2,1,0:T(8,128)S(1)} %bitcast.359, f32[16,2,16,1024]{3,2,1,0:T(8,128)S(1)} %get-tuple-element.24, f32[16,2,16,1024]{3,2,1,0:T(8,128)S(1)} %get-tuple-element.23, f32[16,2,16,1023]{3,2,1,0:T(8,128)S(1)} %bitcast.358, ...), kind=kLoop, calls=%fused_computation.29 | loop fusion | flops 6815744 | bytes 21690368 | tf_op jit(solution)/shard_map/add | solution.py:137
  86.0 0.6 slice.456
  86.7 1.9 %pad_maximum_fusion.1 = f32[16,2,16,1024]{3,2,1,0:T(8,128)} fusion(f32[16,2,16,992]{3,2,1,0:T(8,128)S(1)} %slice.456, f32[16,2,16,32]{3,2,1,0:T(8,128)S(1)} %slice_add_fusion.1), kind=kLoop, calls=%fused_computation.35 | loop fusion | flops 524288 | bytes 4194304 | tf_op jit(solution)/shard_map/concatenate | solution.py:140
  (66 shorter events, 1.6 us)
Async XLA Ops:
  0.0 10.8 %copy-start = (f32[4,2,16,1024]{3,2,1,0:T(8,128)S(1)}, f32[4,2,16,1024]{3,2,1,0:T(8,128)}, u32[]{:S(2)}) copy-start(f32[4,2,16,1024]{3,2,1,0:T(8,128)} %param.10) | copy-start | bytes 1572868
  2.6 43.2 %collective-permute-start.2 = (f32[4,3168]{1,0:T(4,128)S(1)}, f32[4,3168]{1,0:T(4,128)S(1)}, u32[]{:S(2)}, u32[]{:S(2)}) collective-permute-start(f32[4,3168]{1,0:T(4,128)S(1)} %get-tuple-element.37), channel_id=1, source_target_pairs={{0,16},{16,32},{32,48},{48,64},{64,80},{80,96},{96,112},{112,128},... | collective-permute-start | bytes 152072 | tf_op jit(solution)/shard_map/ppermute | solution.py:25
  4.7 41.1 %collective-permute-start.3 = (f32[4,3168]{1,0:T(4,128)S(1)}, f32[4,3168]{1,0:T(4,128)S(1)}, u32[]{:S(2)}, u32[]{:S(2)}) collective-permute-start(f32[4,3168]{1,0:T(4,128)S(1)} %get-tuple-element.38), channel_id=1, source_target_pairs={{16,0},{32,16},{48,32},{64,48},{80,64},{96,80},{112,96},{128,112},... | collective-permute-start | bytes 152072 | tf_op jit(solution)/shard_map/ppermute | solution.py:27
  36.5 5.6 %collective-permute-start.4 = (f32[2,4,64]{2,1,0:T(4,128)S(1)}, f32[2,4,64]{2,1,0:T(4,128)S(1)}, u32[]{:S(2)}, u32[]{:S(2)}) collective-permute-start(f32[2,4,64]{2,1,0:T(4,128)S(1)} %get-tuple-element.43), channel_id=1, source_target_pairs={{0,16},{16,32},{32,48},{48,64},{64,80},{80,96},{96,112},{112,128},... | collective-permute-start | bytes 6152 | tf_op jit(solution)/shard_map/ppermute | solution.py:25
  36.6 9.1 %collective-permute-start.5 = (f32[2,4,64]{2,1,0:T(4,128)S(1)}, f32[2,4,64]{2,1,0:T(4,128)S(1)}, u32[]{:S(2)}, u32[]{:S(2)}) collective-permute-start(f32[2,4,64]{2,1,0:T(4,128)S(1)} %get-tuple-element.44), channel_id=1, source_target_pairs={{16,0},{32,16},{48,32},{64,48},{80,64},{96,80},{112,96},{128,112},... | collective-permute-start | bytes 6152 | tf_op jit(solution)/shard_map/ppermute | solution.py:27
  41.9 22.0 %collective-permute-start = (f32[16,2,4,1024]{3,2,0,1:T(4,128)S(1)}, f32[16,2,4,1024]{3,2,0,1:T(4,128)S(1)}, u32[]{:S(2)}, u32[]{:S(2)}) collective-permute-start(f32[16,2,4,1024]{3,2,0,1:T(4,128)S(1)} %get-tuple-element.28), channel_id=1, source_target_pairs={{0,16},{16,32},{32,48},{48,64},{64,80},{80,96},{96,112},{112,128},... | collective-permute-start | bytes 1572872 | tf_op jit(solution)/shard_map/ppermute | solution.py:25
  42.0 24.1 %collective-permute-start.1 = (f32[16,2,4,1024]{3,2,0,1:T(4,128)S(1)}, f32[16,2,4,1024]{3,2,0,1:T(4,128)S(1)}, u32[]{:S(2)}, u32[]{:S(2)}) collective-permute-start(f32[16,2,4,1024]{3,2,0,1:T(4,128)S(1)} %get-tuple-element.29), channel_id=1, source_target_pairs={{16,0},{32,16},{48,32},{64,48},{80,64},{96,80},{112,96},{128,112},... | collective-permute-start | bytes 1572872 | tf_op jit(solution)/shard_map/ppermute | solution.py:27
  46.0 20.1 %copy-start.1 = (f32[16,2,16,1024]{3,2,1,0:T(8,128)S(1)}, f32[16,2,16,1024]{3,2,1,0:T(8,128)}, u32[]{:S(2)}) copy-start(f32[16,2,16,1024]{3,2,1,0:T(8,128)} %param.9) | copy-start | bytes 6291460
  68.3 2.9 %copy-start.2 = (f32[20,1024]{1,0:T(8,128)S(1)}, f32[20,1024]{1,0:T(8,128)}, u32[]{:S(2)}) copy-start(f32[20,1024]{1,0:T(8,128)} %get-tuple-element.52) | copy-start | bytes 245764
  68.3 2.9 %copy-start.3 = (f32[20,1024]{1,0:T(8,128)S(1)}, f32[20,1024]{1,0:T(8,128)}, u32[]{:S(2)}) copy-start(f32[20,1024]{1,0:T(8,128)} %get-tuple-element.45) | copy-start | bytes 245764
  68.4 2.9 %copy-start.4 = (f32[20,1024]{1,0:T(8,128)S(1)}, f32[20,1024]{1,0:T(8,128)}, u32[]{:S(2)}) copy-start(f32[20,1024]{1,0:T(8,128)} %get-tuple-element.46) | copy-start | bytes 245764
  79.8 1.8 %copy-start.5 = (f32[16,1024]{1,0:T(8,128)S(1)}, f32[16,1024]{1,0:T(8,128)}, u32[]{:S(2)}) copy-start(f32[16,1024]{1,0:T(8,128)} %slice.448) | copy-start | bytes 196612
  79.8 1.8 %copy-start.6 = (f32[16,1024]{1,0:T(8,128)S(1)}, f32[16,1024]{1,0:T(8,128)}, u32[]{:S(2)}) copy-start(f32[16,1024]{1,0:T(8,128)} %slice.450) | copy-start | bytes 196612
  81.6 1.9 %copy-start.7 = (f32[16,1024]{1,0:T(8,128)S(1)}, f32[16,1024]{1,0:T(8,128)}, u32[]{:S(2)}) copy-start(f32[16,1024]{1,0:T(8,128)} %get-tuple-element.55) | copy-start | bytes 196612
  81.6 1.9 %copy-start.8 = (f32[16,1024]{1,0:T(8,128)S(1)}, f32[16,1024]{1,0:T(8,128)}, u32[]{:S(2)}) copy-start(f32[16,1024]{1,0:T(8,128)} %get-tuple-element.56) | copy-start | bytes 196612
  81.6 1.9 %copy-start.9 = (f32[16,1024]{1,0:T(8,128)S(1)}, f32[16,1024]{1,0:T(8,128)}, u32[]{:S(2)}) copy-start(f32[16,1024]{1,0:T(8,128)} %get-tuple-element.47) | copy-start | bytes 196612
  81.6 1.9 %copy-start.10 = (f32[16,1024]{1,0:T(8,128)S(1)}, f32[16,1024]{1,0:T(8,128)}, u32[]{:S(2)}) copy-start(f32[16,1024]{1,0:T(8,128)} %get-tuple-element.48) | copy-start | bytes 196612
